TPU v7x, 256 devices: a whole 4x4x8 slice. The times are simulated.
256 devices in a mesh: gx: 16 (over z_lo, x, core), gy: 16 (over z_hi, y).
Axes of the slice: x: 4, y: 4, z: 8 (z_hi: 4, z_lo: 2; z = z_hi * 2 + z_lo), core: 2. Of those that a mesh axis runs over, the one named last changes fastest.
Arguments:
- species_field: float32 [4, 1024, 256, 256], P(None, 'gx', 'gy'), may hold values from -400 to 400
- initial: float32 [1024, 128], replicated, may hold values from -6 to 6
Outputs:
- factor: float32 [1024, 128], replicated
- gram_two: float32 [256, 256], replicated
All inputs are finite; a program needn't handle non-finite values.
Results may differ from a plain program's by a relative error of at most 0.0002.
Values sent between devices are 32-bit elements; how exact they have to be, the bound alone decides.
No kernel may reach another device: no remote copies, remote signals or barrier semaphores. Data moves between devices by JAX's collectives and lax.ppermute only.
A program may use at most 128 MiB of HBM per device.

v0:
```python
import math
import jax
import jax.numpy as jnp
from jax import lax
from jax.sharding import PartitionSpec as P

S = 4
NY = 256
NZ = 256
R = 128
SWEEPS = 3


def body(species_field, initial):
    highest = lax.Precision.HIGHEST
    regrouped = lax.all_to_all(species_field, "gx", split_axis=3, concat_axis=1, tiled=True)
    species, rows_x, cols_y, slab_z = regrouped.shape
    fibers = regrouped.reshape(species, rows_x, cols_y * slab_z)
    scale_one = 1.0 / (S * NY * NZ)
    basis = initial
    gram_one = lax.psum(
        jnp.einsum("sxc,swc->xw", fibers, fibers, precision=highest) * scale_one, ("gx", "gy")
    )
    for sweep_index in range(SWEEPS):
        wide = jnp.dot(gram_one, basis, precision=highest, preferred_element_type=jnp.float32)
        square = jnp.dot(wide.T, wide, precision=highest, preferred_element_type=jnp.float32)
        factor_low = jnp.linalg.cholesky(square)
        basis = jax.scipy.linalg.solve_triangular(factor_low, wide.T, lower=True).T
    core_tensor = jnp.einsum("xr,sxc->src", basis, fibers, precision=highest)
    core_blocks = core_tensor.reshape(species, R, cols_y, slab_z)
    blocks = lax.all_to_all(core_blocks, "gy", split_axis=1, concat_axis=2, tiled=True)
    second_part = jnp.einsum("sryz,srwz->yw", blocks, blocks, precision=highest) / (S * R * NZ)
    gram_two = lax.psum(second_part, ("gx", "gy"))
    return (basis * math.sqrt(rows_x), gram_two)


def solution(mesh):
    placed = (P(None, "gx", "gy", None), P())
    return jax.shard_map(body, mesh=mesh, in_specs=placed, out_specs=(P(), P()), check_vma=False)
```

profile of v0, /device:TPU:2, one launch (start us, length us, event | category | flops | bytes accessed | tf_op | source)
XLA Modules:
  0.0 817.2 jit_solution(10671262008300448773)
XLA Ops:
  7.2 9.2 %copy.33 = f32[4,64,16,256]{1,2,0,3:T(8,128)} copy(f32[4,64,16,256]{3,2,1,0:T(8,128)} %param.5) | data formatting | bytes 8388608 | tf_op args[0]
  16.4 13.3 %reshape.24 = f32[16,1,65536]{2,1,0:T(1,128)} reshape(f32[256,4,16,64]{3,2,1,0:T(8,128)} %bitcast.87) | data formatting | bytes 8388608
  29.7 53.2 %all_to_all.33 = f32[16,1,65536]{2,1,0:T(1,128)} all-to-all(f32[16,1,65536]{2,1,0:T(1,128)} %reshape.24), channel_id=1, replica_groups=mesh['gx'=16,'gy'=16] {'gx'}, dimensions={0} | all-to-all | bytes 8388608 | tf_op jit(solution)/shard_map/all_to_all | solution.py:16
  82.9 0.5 broadcast.39
  83.4 13.7 %reduce.4 = f32[16,65536]{1,0:T(8,128)} reduce(f32[16,1,65536]{2,1,0:T(1,128)} %all_to_all.33, f32[]{:T(128)} %broadcast.39), dimensions={1}, to_apply=%all_to_all.24.reduce_sub_computation | reduce | bytes 8388612 | tf_op jit(solution)/shard_map/all_to_all | solution.py:16
  97.2 6.9 reshape.25
  104.1 11.4 %copy.35 = f32[4,16,64,16,16]{2,1,4,3,0:T(8,128)} copy(f32[4,16,64,16,16]{2,3,0,4,1:T(8,128)} %bitcast.88) | data formatting | bytes 8388608 | tf_op jit(solution)/shard_map/all_to_all | solution.py:16
  115.5 7.6 reshape.19
  123.1 17.8 %bitcast_multiply_fusion = f32[1024,1024]{1,0:T(8,128)} fusion(f32[4,1024,256]{1,2,0:T(8,128)} %reshape.19), kind=kOutput, calls=%fused_computation | convolution fusion | flops 12885950464 | bytes 8388608 | tf_op jit(solution)/shard_map/sxc,swc->xw/dot_general | solution.py:22
  140.9 0.0 all-reduce.5.cloned.1.call-start
  141.0 273.0 %all-reduce.3.cloned.1.call-done = f32[1024,1024]{1,0:T(8,128)} async-done(((f32[1024,1024]{1,0:T(8,128)}), f32[1024,1024]{1,0:T(8,128)}) %all-reduce.3.cloned.1.call-update) | async-done | bytes 4194320 | tf_op jit(solution)/shard_map/psum | solution.py:21
  414.0 5.6 fusion.21
  419.6 1.0 fusion.22
  420.6 0.1 copy.38
  420.7 11.7 %cholesky.59 = f32[128,128]{1,0:T(8,128)S(1)} custom-call(f32[128,128]{1,0:T(8,128)S(1)} %fusion.16), custom_call_target="Cholesky" | custom-call | tf_op jit(solution)/shard_map/jit(cholesky)/cholesky | solution.py:27
  432.5 0.6 compare_reduce_fusion.2
  433.1 0.7 fusion.8
  433.8 9.8 %custom-call.7 = f32[1,128,128]{1,2,0:T(8,128)S(1)} custom-call(f32[1,128,128]{2,1,0:T(8,128)S(1)} %fusion.8), custom_call_target="InvertDiagBlocksLowerTriangular" | custom-call | tf_op jit(solution)/shard_map/jit(_solve_triangular)/triangular_solve | solution.py:28
  443.6 0.6 fusion.6
  444.2 5.4 fusion.23
  449.7 1.0 fusion.24
  450.7 0.1 copy.39
  450.8 11.7 %cholesky.70 = f32[128,128]{1,0:T(8,128)S(1)} custom-call(f32[128,128]{1,0:T(8,128)S(1)} %fusion.14), custom_call_target="Cholesky" | custom-call | tf_op jit(solution)/shard_map/jit(cholesky)/cholesky | solution.py:27
  462.5 0.6 compare_reduce_fusion.1
  463.2 0.7 fusion.9
  463.8 9.8 %custom-call.8 = f32[1,128,128]{1,2,0:T(8,128)S(1)} custom-call(f32[1,128,128]{2,1,0:T(8,128)S(1)} %fusion.9), custom_call_target="InvertDiagBlocksLowerTriangular" | custom-call | tf_op jit(solution)/shard_map/jit(_solve_triangular)/triangular_solve | solution.py:28
  473.7 0.6 fusion.4
  474.3 5.4 fusion.25
  479.7 1.0 fusion.26
  480.7 0.1 copy.40
  480.9 11.7 %cholesky.81 = f32[128,128]{1,0:T(8,128)S(1)} custom-call(f32[128,128]{1,0:T(8,128)S(1)} %fusion.12), custom_call_target="Cholesky" | custom-call | tf_op jit(solution)/shard_map/jit(cholesky)/cholesky | solution.py:27
  492.6 0.6 compare_reduce_fusion
  493.3 0.7 fusion.10
  493.9 9.8 %custom-call.9 = f32[1,128,128]{1,2,0:T(8,128)S(1)} custom-call(f32[1,128,128]{2,1,0:T(8,128)S(1)} %fusion.10), custom_call_target="InvertDiagBlocksLowerTriangular" | custom-call | tf_op jit(solution)/shard_map/jit(_solve_triangular)/triangular_solve | solution.py:28
  503.7 0.6 fusion.2
  504.4 6.5 convolution_bitcast_fusion
  510.9 0.2 copy.42
  511.1 4.6 copy.43
  515.8 3.5 reshape.26
  519.3 20.9 %all_to_all.34 = f32[16,1,8192]{2,1,0:T(1,128)S(1)} all-to-all(f32[16,1,8192]{2,1,0:T(1,128)S(1)} %reshape.26), channel_id=1, replica_groups=mesh['gx'=16,'gy'=16] {'gy'}, dimensions={0} | all-to-all | bytes 1048576 | tf_op jit(solution)/shard_map/all_to_all | solution.py:31
  540.2 1.9 reduce.5
  542.1 2.8 reshape.27
  544.9 5.6 copy.45
  550.4 3.5 all_to_all.30
  553.9 1.7 fusion
  555.7 1.0 copy.46
  556.7 251.5 %all-reduce.5.cloned.1.call-done = f32[256,256]{1,0:T(8,128)} async-done(((f32[256,256]{1,0:T(8,128)}), f32[256,256]{1,0:T(8,128)}) %all-reduce.5.cloned.1.call-update) | async-done | bytes 262160 | tf_op jit(solution)/shard_map/psum | solution.py:33
  808.3 1.7 copy.55
  (12 shorter events, 0.3 us)
Async XLA Ops:
  7.2 406.8 %copy-start = (f32[1024,128]{1,0:T(8,128)S(1)}, f32[1024,128]{1,0:T(8,128)}, u32[]{:S(2)}) copy-start(f32[1024,128]{1,0:T(8,128)} %param.6) | copy-start | bytes 1572868
  7.2 406.8 %all-reduce.3.cloned.1.call-start = ((), (), s32[]{:S(2)}) async-start(), calls=%async_computation.2 | async-start | bytes 8388608 | tf_op jit(solution)/shard_map/psum | solution.py:21
  140.9 667.4 %all-reduce.5.cloned.1.call-start = ((), (), s32[]{:S(2)}) async-start(), calls=%async_computation.3 | async-start | bytes 524288 | tf_op jit(solution)/shard_map/psum | solution.py:33
Sparse Core Ops, SparseCore 0:
  141.0 272.9 all-reduce.2
  555.8 252.4 all-reduce.4
where the time goes:
time: 826 us; the launch traced here: 817 us
  waiting for transfers between devices  525 us (64%)
  other arithmetic  84.2 us (10%)
  blocking collectives  74.2 us (9%)
  local copies, waits for them, and re-layouts  72 us (9%)
  matrix products  47.4 us (6%)
  between operations  14.7 us (2%)
    psum x1, waiting for transfers between devices, body(): lax.psum(jnp.einsum('sxc,swc->xw', fibers, fibers, precision=highest) * s...  273 us
    psum x1, waiting for transfers between devices, body(): gram_two = lax.psum(second_part, ('gx', 'gy'))  252 us
    all_to_all x1, blocking collectives, body(): lax.all_to_all(species_field, 'gx', split_axis=3, concat_axis=1, tiled=True)  53.2 us
    unnamed x9, local copies, waits for them, and re-layouts  38.3 us
    another operation x9, other arithmetic, body(): factor_low = jnp.linalg.cholesky(square)  37.2 us
    another operation x6, other arithmetic, body(): basis = jax.scipy.linalg.solve_triangular(factor_low, wide.T, lower=True).T  31.4 us
    all_to_all x1, blocking collectives, body(): lax.all_to_all(core_blocks, 'gy', split_axis=1, concat_axis=2, tiled=True)  20.9 us
    dot_general x1, matrix products, body(): jnp.einsum('sxc,swc->xw', fibers, fibers, precision=highest) * scale_one  17.8 us
  transfers between devices with their start and end apart: 2, of which 2 were waited for; matrix products, arithmetic and copies ran while one was open for 0% of the time, Pallas kernels for 0%

commit v1 on v0

--- a/solution.py
+++ b/solution.py
@@ -13,7 +13,12 @@
 
 def body(species_field, initial):
     highest = lax.Precision.HIGHEST
-    regrouped = lax.all_to_all(species_field, "gx", split_axis=3, concat_axis=1, tiled=True)
+    regrouped = jnp.concatenate(
+        jax.lax.all_to_all(
+            jnp.stack(jnp.split(species_field, jax.lax.axis_size("gx"), axis=3), axis=0), "gx", 0, 0
+        ),
+        axis=1,
+    )
     species, rows_x, cols_y, slab_z = regrouped.shape
     fibers = regrouped.reshape(species, rows_x, cols_y * slab_z)
     scale_one = 1.0 / (S * NY * NZ)

time: 826 us -> 916 us (1.11)
  local copies, waits for them, and re-layouts: 72 us -> 168 us
    unnamed x9 -> x61, local copies, waits for them, and re-layouts: 38.3 us -> 106 us
    split x0 -> x1, local copies, waits for them, and re-layouts: none -> 26.9 us  [body(): jnp.split(species_field, jax.lax.axis_size('gx'), axis=3)]
    all_to_all x2 -> x1, local copies, waits for them, and re-layouts: 12 us -> 0.51 us  [body(): jax.lax.all_to_all(jnp.stack(jnp.split(species_field, jax.lax.axis_size('...]
where the time goes in v1:
time: 916 us; the launch traced here: 912 us
  waiting for transfers between devices  525 us (57%)
  local copies, waits for them, and re-layouts  168 us (18%)
  other arithmetic  84.2 us (9%)
  blocking collectives  74.4 us (8%)
  matrix products  45.9 us (5%)
  between operations  14.6 us (2%)
    psum x1, waiting for transfers between devices, body(): lax.psum(jnp.einsum('sxc,swc->xw', fibers, fibers, precision=highest) * s...  273 us
    psum x1, waiting for transfers between devices, body(): gram_two = lax.psum(second_part, ('gx', 'gy'))  252 us
    unnamed x61, local copies, waits for them, and re-layouts  106 us
    all_to_all x1, blocking collectives, body(): jax.lax.all_to_all(jnp.stack(jnp.split(species_field, jax.lax.axis_size('...  53.2 us
    another operation x9, other arithmetic, body(): factor_low = jnp.linalg.cholesky(square)  37.2 us
    another operation x6, other arithmetic, body(): basis = jax.scipy.linalg.solve_triangular(factor_low, wide.T, lower=True).T  31.4 us
    split x1, local copies, waits for them, and re-layouts, body(): jnp.split(species_field, jax.lax.axis_size('gx'), axis=3)  26.9 us
    all_to_all x1, blocking collectives, body(): lax.all_to_all(core_blocks, 'gy', split_axis=1, concat_axis=2, tiled=True)  21.2 us
  transfers between devices with their start and end apart: 2, of which 2 were waited for; matrix products, arithmetic and copies ran while one was open for 0% of the time, Pallas kernels for 0%

profile of v1, /device:TPU:2, one launch (start us, length us, event | category | flops | bytes accessed | tf_op | source)
XLA Modules:
  0.0 911.9 jit_solution(3556157632553061985)
XLA Ops:
  7.2 26.9 %fusion.22 = (f32[4,64,16,16]{3,2,1,0:T(8,128)}, f32[4,64,16,16]{3,2,1,0:T(8,128)}, f32[4,64,16,16]{3,2,1,0:T(8,128)}, f32[4,64,16,16]{3,2,1,0:T(8,128)}, f32[4,...) fusion(f32[4,64,16,256]{3,2,1,0:T(8,128)} %param.5), kind=kLoop, calls=%fused_computation.53 | loop fusion | bytes 8388608 | tf_op jit(solution)/shard_map/split | solution.py:18
  34.2 2.3 copy.65
  36.5 3.1 copy.64
  39.6 3.2 copy.63
  42.8 3.1 copy.62
  45.9 3.1 copy.61
  49.0 3.1 copy.60
  52.2 3.1 copy.59
  55.3 3.1 copy.58
  58.4 3.1 copy.57
  61.5 3.1 copy.56
  64.7 3.1 copy.55
  67.8 3.1 copy.54
  70.9 3.1 copy.53
  74.0 3.1 copy.52
  77.2 3.1 copy.51
  81.9 2.0 bitcast_dynamic-update-slice_fusion.15
  83.9 1.9 bitcast_dynamic-update-slice_fusion.14
  85.8 1.9 bitcast_dynamic-update-slice_fusion.13
  87.8 14.4 %bitcast_dynamic-update-slice_fusion.12 = f32[16,4,64,16,16]{2,4,3,1,0:T(8,128)} fusion(f32[16,4,64,16,16]{2,4,3,1,0:T(8,128)} %bitcast_dynamic-update-slice_fusion.13, f32[4,64,16,16]{1,3,2,0:T(8,128)} %copy.53), kind=kLoop, calls=%fused_computation.23 | loop fusion | bytes 1048576
  112.3 13.3 %reshape.23 = f32[16,1,65536]{2,1,0:T(1,128)} reshape(f32[16,4,16,16,64]{4,3,2,1,0:T(8,128)} %bitcast.96) | data formatting | bytes 8388608
  125.6 53.2 %all_to_all.23 = f32[16,1,65536]{2,1,0:T(1,128)} all-to-all(f32[16,1,65536]{2,1,0:T(1,128)} %reshape.23), channel_id=1, replica_groups=mesh['gx'=16,'gy'=16] {'gx'}, dimensions={0} | all-to-all | bytes 8388608 | tf_op jit(solution)/shard_map/all_to_all | solution.py:17
  179.4 13.7 %reduce.4 = f32[16,65536]{1,0:T(8,128)} reduce(f32[16,1,65536]{2,1,0:T(1,128)} %all_to_all.23, f32[]{:T(128)} %broadcast.39), dimensions={1}, to_apply=%all_to_all.16.reduce_sub_computation | reduce | bytes 8388612 | tf_op jit(solution)/shard_map/all_to_all | solution.py:17
  193.1 6.9 reshape.24
  200.0 3.9 bitcast_bitcast_fusion
  203.9 8.1 copy.36
  212.0 7.6 reshape_reshape.3
  219.6 17.6 %bitcast_multiply_fusion = f32[1024,1024]{1,0:T(8,128)} fusion(f32[4,1024,256]{1,2,0:T(8,128)} %reshape_reshape.3), kind=kOutput, calls=%fused_computation | convolution fusion | flops 12885950464 | bytes 8388608 | tf_op jit(solution)/shard_map/sxc,swc->xw/dot_general | solution.py:27
  237.3 273.0 %all-reduce.3.cloned.1.call-done = f32[1024,1024]{1,0:T(8,128)} async-done(((f32[1024,1024]{1,0:T(8,128)}), f32[1024,1024]{1,0:T(8,128)}) %all-reduce.3.cloned.1.call-update) | async-done | bytes 4194320 | tf_op jit(solution)/shard_map/psum | solution.py:26
  510.3 5.6 fusion.23
  517.0 11.7 %cholesky.59 = f32[128,128]{1,0:T(8,128)S(1)} custom-call(f32[128,128]{1,0:T(8,128)S(1)} %fusion.17), custom_call_target="Cholesky" | custom-call | tf_op jit(solution)/shard_map/jit(cholesky)/cholesky | solution.py:32
  530.0 9.8 %custom-call.7 = f32[1,128,128]{1,2,0:T(8,128)S(1)} custom-call(f32[1,128,128]{2,1,0:T(8,128)S(1)} %fusion.9), custom_call_target="InvertDiagBlocksLowerTriangular" | custom-call | tf_op jit(solution)/shard_map/jit(_solve_triangular)/triangular_solve | solution.py:33
  540.5 5.4 fusion.25
  547.0 11.7 %cholesky.70 = f32[128,128]{1,0:T(8,128)S(1)} custom-call(f32[128,128]{1,0:T(8,128)S(1)} %fusion.15), custom_call_target="Cholesky" | custom-call | tf_op jit(solution)/shard_map/jit(cholesky)/cholesky | solution.py:32
  560.1 9.8 %custom-call.8 = f32[1,128,128]{1,2,0:T(8,128)S(1)} custom-call(f32[1,128,128]{2,1,0:T(8,128)S(1)} %fusion.10), custom_call_target="InvertDiagBlocksLowerTriangular" | custom-call | tf_op jit(solution)/shard_map/jit(_solve_triangular)/triangular_solve | solution.py:33
  570.6 5.4 fusion.27
  577.1 11.7 %cholesky.81 = f32[128,128]{1,0:T(8,128)S(1)} custom-call(f32[128,128]{1,0:T(8,128)S(1)} %fusion.13), custom_call_target="Cholesky" | custom-call | tf_op jit(solution)/shard_map/jit(cholesky)/cholesky | solution.py:32
  590.2 9.8 %custom-call.9 = f32[1,128,128]{1,2,0:T(8,128)S(1)} custom-call(f32[1,128,128]{2,1,0:T(8,128)S(1)} %fusion.11), custom_call_target="InvertDiagBlocksLowerTriangular" | custom-call | tf_op jit(solution)/shard_map/jit(_solve_triangular)/triangular_solve | solution.py:33
  600.6 5.2 fusion.1
  605.9 4.4 copy.42
  610.3 3.5 reshape.25
  613.8 21.2 %all_to_all.24 = f32[16,1,8192]{2,1,0:T(1,128)S(1)} all-to-all(f32[16,1,8192]{2,1,0:T(1,128)S(1)} %reshape.25), channel_id=1, replica_groups=mesh['gx'=16,'gy'=16] {'gy'}, dimensions={0} | all-to-all | bytes 1048576 | tf_op jit(solution)/shard_map/all_to_all | solution.py:36
  635.0 1.9 reduce.5
  636.9 2.8 reshape.26
  639.6 5.6 copy.44
  645.2 3.5 all_to_all.20
  648.7 1.7 fusion
  651.5 251.6 %all-reduce.5.cloned.1.call-done = f32[256,256]{1,0:T(8,128)} async-done(((f32[256,256]{1,0:T(8,128)}), f32[256,256]{1,0:T(8,128)}) %all-reduce.5.cloned.1.call-update) | async-done | bytes 262160 | tf_op jit(solution)/shard_map/psum | solution.py:38
  (66 shorter events, 24.3 us)
Async XLA Ops:
  7.2 503.1 %copy-start = (f32[1024,128]{1,0:T(8,128)S(1)}, f32[1024,128]{1,0:T(8,128)}, u32[]{:S(2)}) copy-start(f32[1024,128]{1,0:T(8,128)} %param.6) | copy-start | bytes 1572868
  7.2 503.1 %all-reduce.3.cloned.1.call-start = ((), (), s32[]{:S(2)}) async-start(), calls=%async_computation.2 | async-start | bytes 8388608 | tf_op jit(solution)/shard_map/psum | solution.py:26
  81.9 20.3 %copy-start.11 = (f32[4,64,16,16]{1,3,2,0:T(8,128)S(1)}, f32[4,64,16,16]{1,3,2,0:T(8,128)}, u32[]{:S(2)}) copy-start(f32[4,64,16,16]{1,3,2,0:T(8,128)} %copy.54) | copy-start | bytes 786436
  81.9 21.1 %copy-start.10 = (f32[4,64,16,16]{1,3,2,0:T(8,128)S(1)}, f32[4,64,16,16]{1,3,2,0:T(8,128)}, u32[]{:S(2)}) copy-start(f32[4,64,16,16]{1,3,2,0:T(8,128)} %copy.55) | copy-start | bytes 786436
  81.9 22.0 %copy-start.9 = (f32[4,64,16,16]{1,3,2,0:T(8,128)S(1)}, f32[4,64,16,16]{1,3,2,0:T(8,128)}, u32[]{:S(2)}) copy-start(f32[4,64,16,16]{1,3,2,0:T(8,128)} %copy.56) | copy-start | bytes 786436
  81.9 22.8 %copy-start.8 = (f32[4,64,16,16]{1,3,2,0:T(8,128)S(1)}, f32[4,64,16,16]{1,3,2,0:T(8,128)}, u32[]{:S(2)}) copy-start(f32[4,64,16,16]{1,3,2,0:T(8,128)} %copy.57) | copy-start | bytes 786436
  81.9 23.7 %copy-start.7 = (f32[4,64,16,16]{1,3,2,0:T(8,128)S(1)}, f32[4,64,16,16]{1,3,2,0:T(8,128)}, u32[]{:S(2)}) copy-start(f32[4,64,16,16]{1,3,2,0:T(8,128)} %copy.58) | copy-start | bytes 786436
  83.9 22.5 %copy-start.6 = (f32[4,64,16,16]{1,3,2,0:T(8,128)S(1)}, f32[4,64,16,16]{1,3,2,0:T(8,128)}, u32[]{:S(2)}) copy-start(f32[4,64,16,16]{1,3,2,0:T(8,128)} %copy.59) | copy-start | bytes 786436
  85.8 21.4 %copy-start.5 = (f32[4,64,16,16]{1,3,2,0:T(8,128)S(1)}, f32[4,64,16,16]{1,3,2,0:T(8,128)}, u32[]{:S(2)}) copy-start(f32[4,64,16,16]{1,3,2,0:T(8,128)} %copy.60) | copy-start | bytes 786436
  87.8 20.3 %copy-start.4 = (f32[4,64,16,16]{1,3,2,0:T(8,128)S(1)}, f32[4,64,16,16]{1,3,2,0:T(8,128)}, u32[]{:S(2)}) copy-start(f32[4,64,16,16]{1,3,2,0:T(8,128)} %copy.61) | copy-start | bytes 786436
  102.2 6.8 copy-start.3
  103.0 6.8 copy-start.2
  103.9 6.8 copy-start.1
  237.2 665.9 %all-reduce.5.cloned.1.call-start = ((), (), s32[]{:S(2)}) async-start(), calls=%async_computation.3 | async-start | bytes 524288 | tf_op jit(solution)/shard_map/psum | solution.py:38
Sparse Core Ops, SparseCore 0:
  237.3 272.8 all-reduce.2
  650.6 252.4 all-reduce.4

commit v2 on v0

--- a/solution.py
+++ b/solution.py
@@ -30,7 +30,7 @@
     core_blocks = core_tensor.reshape(species, R, cols_y, slab_z)
     blocks = lax.all_to_all(core_blocks, "gy", split_axis=1, concat_axis=2, tiled=True)
     second_part = jnp.einsum("sryz,srwz->yw", blocks, blocks, precision=highest) / (S * R * NZ)
-    gram_two = lax.psum(second_part, ("gx", "gy"))
+    gram_two = lax.all_gather(second_part, ("gx", "gy")).sum(axis=0)
     return (basis * math.sqrt(rows_x), gram_two)
 
 

time: 826 us -> 1390 us (1.68)
  waiting for transfers between devices: 525 us -> 1060 us
  other arithmetic: 84.2 us -> 106 us
    all_gather x0 -> x1, waiting for transfers between devices: none -> 786 us  [body(): gram_two = lax.all_gather(second_part, ('gx', 'gy')).sum(axis=0)]
    psum x1 -> x0, waiting for transfers between devices: 252 us -> none  [body(): gram_two = lax.psum(second_part, ('gx', 'gy'))]
    reduce_sum x0 -> x1, other arithmetic: none -> 21.8 us  [body(): gram_two = lax.all_gather(second_part, ('gx', 'gy')).sum(axis=0)]
    unnamed x9 -> x10, local copies, waits for them, and re-layouts: 38.3 us -> 36.6 us
where the time goes in v2:
time: 1390 us; the launch traced here: 1370 us
  waiting for transfers between devices  1060 us (76%)
  other arithmetic  106 us (8%)
  blocking collectives  74.2 us (5%)
  local copies, waits for them, and re-layouts  70.4 us (5%)
  matrix products  47.4 us (3%)
  between operations  14.7 us (1%)
    all_gather x1, waiting for transfers between devices, body(): gram_two = lax.all_gather(second_part, ('gx', 'gy')).sum(axis=0)  786 us
    psum x1, waiting for transfers between devices, body(): lax.psum(jnp.einsum('sxc,swc->xw', fibers, fibers, precision=highest) * s...  273 us
    all_to_all x1, blocking collectives, body(): lax.all_to_all(species_field, 'gx', split_axis=3, concat_axis=1, tiled=True)  53.2 us
    another operation x9, other arithmetic, body(): factor_low = jnp.linalg.cholesky(square)  37.2 us
    unnamed x10, local copies, waits for them, and re-layouts  36.6 us
    another operation x6, other arithmetic, body(): basis = jax.scipy.linalg.solve_triangular(factor_low, wide.T, lower=True).T  31.4 us
  transfers between devices with their start and end apart: 2, of which 2 were waited for; matrix products, arithmetic and copies ran while one was open for 0% of the time, Pallas kernels for 0%

profile of v2, /device:TPU:2, one launch (start us, length us, event | category | flops | bytes accessed | tf_op | source)
XLA Modules:
  0.0 1372.0 jit_solution(1374984329752968847)
XLA Ops:
  7.2 9.2 copy.33
  16.4 13.3 reshape.25
  29.7 53.2 %all_to_all.33 = f32[16,1,65536]{2,1,0:T(1,128)} all-to-all(f32[16,1,65536]{2,1,0:T(1,128)} %reshape.25), channel_id=1, replica_groups=mesh['gx'=16,'gy'=16] {'gx'}, dimensions={0} | all-to-all | bytes 8388608 | tf_op jit(solution)/shard_map/all_to_all | solution.py:16
  82.9 0.5 broadcast.39
  83.4 13.7 reduce.4
  97.2 6.9 reshape.26
  104.1 11.4 copy.35
  115.5 7.6 reshape.19
  123.1 17.8 %bitcast_multiply_fusion = f32[1024,1024]{1,0:T(8,128)} fusion(f32[4,1024,256]{1,2,0:T(8,128)} %reshape.19), kind=kOutput, calls=%fused_computation | convolution fusion | flops 12885950464 | bytes 8388608 | tf_op jit(solution)/shard_map/sxc,swc->xw/dot_general | solution.py:22
  140.9 0.0 all-gather.3.cloned.1.call-start
  141.0 273.0 %all-reduce.2.cloned.1.call-done = f32[1024,1024]{1,0:T(8,128)} async-done(((f32[1024,1024]{1,0:T(8,128)}), f32[1024,1024]{1,0:T(8,128)}) %all-reduce.2.cloned.1.call-update) | async-done | bytes 4194320 | tf_op jit(solution)/shard_map/psum | solution.py:21
  414.0 5.6 fusion.21
  419.6 1.0 fusion.22
  420.6 0.1 copy.38
  420.7 11.7 cholesky.59
  432.5 0.6 compare_reduce_fusion.2
  433.1 0.7 fusion.8
  433.8 9.8 custom-call.7
  443.6 0.6 fusion.6
  444.3 5.4 fusion.23
  449.6 1.0 fusion.24
  450.7 0.1 copy.39
  450.8 11.7 cholesky.70
  462.5 0.6 compare_reduce_fusion.1
  463.2 0.7 fusion.9
  463.8 9.8 custom-call.8
  473.6 0.6 fusion.4
  474.3 5.4 fusion.25
  479.7 1.0 fusion.26
  480.8 0.1 copy.40
  480.9 11.7 cholesky.81
  492.6 0.6 compare_reduce_fusion
  493.3 0.7 fusion.10
  493.9 9.8 custom-call.9
  503.7 0.6 fusion.2
  504.4 6.5 convolution_bitcast_fusion
  510.9 0.2 copy.42
  511.1 4.6 copy.43
  515.8 3.5 reshape.27
  519.3 21.0 %all_to_all.34 = f32[16,1,8192]{2,1,0:T(1,128)S(1)} all-to-all(f32[16,1,8192]{2,1,0:T(1,128)S(1)} %reshape.27), channel_id=1, replica_groups=mesh['gx'=16,'gy'=16] {'gy'}, dimensions={0} | all-to-all | bytes 1048576 | tf_op jit(solution)/shard_map/all_to_all | solution.py:31
  540.2 1.9 reduce.5
  542.1 2.8 reshape.28
  544.9 5.6 copy.45
  550.5 3.5 all_to_all.30
  554.0 1.7 fusion
  555.7 1.0 copy.46
  556.7 786.2 %all-gather.3.cloned.1.call-done = f32[65536,256]{1,0:T(8,128)} async-done(((f32[256,256]{1,0:T(8,128)}), f32[65536,256]{1,0:T(8,128)}) %all-gather.3.cloned.1.call-update) | async-done | bytes 67108880 | tf_op jit(solution)/shard_map/all_gather | solution.py:33
  1342.9 21.8 %reduce_sum.9 = f32[256,256]{1,0:T(8,128)} reduce(f32[256,256,256]{2,1,0:T(8,128)} %bitcast.25, f32[]{:T(128)} %constant.39.clone.1), dimensions={0}, to_apply=%region_3.6 | reduce | flops 16711680 | bytes 67371008 | tf_op jit(solution)/shard_map/reduce_sum | solution.py:33
  (14 shorter events, 0.3 us)
Async XLA Ops:
  7.2 406.8 %copy-start = (f32[1024,128]{1,0:T(8,128)S(1)}, f32[1024,128]{1,0:T(8,128)}, u32[]{:S(2)}) copy-start(f32[1024,128]{1,0:T(8,128)} %param.6) | copy-start | bytes 1572868
  7.2 406.8 %all-reduce.2.cloned.1.call-start = ((), (), s32[]{:S(2)}) async-start(), calls=%async_computation.2 | async-start | bytes 8388608 | tf_op jit(solution)/shard_map/psum | solution.py:21
  140.9 1202.0 %all-gather.3.cloned.1.call-start = ((), (), s32[]{:S(2)}) async-start(), calls=%async_computation.3 | async-start | bytes 67371008 | tf_op jit(solution)/shard_map/all_gather | solution.py:33
  1342.9 21.8 %copy-start.1 = (f32[1024,128]{1,0:T(8,128)S(1)}, f32[1024,128]{1,0:T(8,128)}, u32[]{:S(2)}) copy-start(f32[1024,128]{1,0:T(8,128)} %param.6) | copy-start | bytes 1572868
Sparse Core Ops, SparseCore 0:
  141.0 272.9 all-reduce.1
  555.8 787.0 all-gather.2
